TPU v7x, 256 devices: a whole 4x4x8 slice. The times are simulated.
256 devices in a mesh: tm: 16 (over y, x), space: 16 (over z, core).
Axes of the slice: x: 4, y: 4, z: 8, core: 2. Of those that a mesh axis runs over, the one named last changes fastest.
Arguments:
- stored: bfloat16 [16, 288, 128, 128], P('tm', None, 'space'), may hold values from -6 to 6
- snapshot: int32 [16, 256], P('tm'), may hold values from 0 to 287, as said below
- balance_coef: float32 [128, 128], P('space'), may hold values from 0.5 to 2
- sea_mask: int32 [128, 128], P('space'), may hold values 0 or 1
Outputs:
- merged_basis: bfloat16 [256, 3, 128, 128], P('tm', None, 'space')
Inputs may be any that keep to these rules, and one draw needn't show every extreme that they name: `snapshot`: the 256 indices of one group are distinct.
All inputs are finite; a program needn't handle non-finite values. No bound on the sum of `sea_mask` on one device may be relied on, other than what follows from the above.
Results may differ from a plain program's by a relative error of at most 0.04.
Values may be sent and summed in bfloat16 or wider, within the bound.
No kernel may reach another device: no remote copies, remote signals or barrier semaphores. Data moves between devices by JAX's collectives and lax.ppermute only.
A program may use at most 64 MiB of HBM per device.

v0:
```python
import jax
import jax.numpy as jnp
from jax import lax
from jax.sharding import PartitionSpec as P

inv_root2 = 0.7071067811865476


def gathered_total(shard, axis):
    return lax.all_gather(shard, axis).astype(jnp.float32).sum(0)


def with_halo(cells, sides, width):
    for axis, dim in sides:
        count = lax.axis_size(axis)
        ends = count - 1
        head = lax.slice_in_dim(cells, 0, width, axis=dim)
        tail = lax.slice_in_dim(cells, cells.shape[dim] - width, cells.shape[dim], axis=dim)
        cells = jnp.concatenate(
            [
                lax.ppermute(tail, axis, [(i, (i + 1) % count) for i in range(ends)]),
                cells,
                lax.ppermute(head, axis, [((i + 1) % count, i) for i in range(ends)]),
            ],
            axis=dim,
        )
    return cells


def from_partner(shard, axis, stride):
    return lax.ppermute(shard, axis, [(i, i ^ 1 << stride) for i in range(lax.axis_size(axis))])


def balance(padded, balance_coef, sea_float):
    center = padded[:, 1:-1, :]
    values = center.astype(jnp.float32)
    east_cells = jnp.roll(values, -1, axis=2)
    west_cells = jnp.roll(values, 1, axis=2)
    zonal_flow = (-balance_coef * sea_float * (east_cells - west_cells)).astype(jnp.bfloat16)
    wide = padded.astype(jnp.float32)
    merid_flow = (balance_coef * sea_float * (wide[:, 2:, :] - wide[:, :-2, :])).astype(
        jnp.bfloat16
    )
    return jnp.stack([center, zonal_flow, merid_flow], axis=1).reshape(center.shape[0], -1)


def stack_pair(own_basis, other_basis, level_idx):
    own_bit = lax.axis_index("tm") // 2**level_idx % 2
    upper_part = jnp.where(own_bit == 0, own_basis, other_basis)
    lower_part = jnp.where(own_bit == 0, other_basis, own_basis)
    return jnp.concatenate([upper_part, lower_part], axis=0)


def merge_pair(own_basis, other_basis, level_idx, last_level):
    stacked = stack_pair(own_basis, other_basis, level_idx)
    members = own_basis.shape[0]
    local_gram = jnp.dot(stacked, stacked.T, preferred_element_type=jnp.float32)
    local_mixed = (local_gram[:, :members] + local_gram[:, members:]) * inv_root2
    mixed_cols = lax.psum(local_mixed, "space")
    normal = jnp.dot(
        mixed_cols.T,
        mixed_cols,
        precision=lax.Precision.HIGHEST,
        preferred_element_type=jnp.float32,
    )
    factor_low = jnp.linalg.cholesky(normal)
    rotation = (
        jax.scipy.linalg.solve_triangular(factor_low, mixed_cols.T, lower=True) * inv_root2
    ).astype(jnp.bfloat16)
    if last_level:
        member_share = rotation.shape[0] // lax.axis_size("tm")
        rotation = lax.dynamic_slice_in_dim(
            rotation, lax.axis_index("tm") * member_share, member_share, 0
        )
    return jnp.dot(rotation, stacked, preferred_element_type=jnp.float32).astype(jnp.bfloat16)


def body(stored, snapshot, balance_coef, sea_mask):
    sea_float = sea_mask.astype(jnp.float32)
    mean_state = jnp.mean(stored[0].astype(jnp.float32), axis=0)
    picked = jnp.take(stored[0], snapshot[0], axis=0)
    anomaly = ((picked.astype(jnp.float32) - mean_state) * sea_float).astype(jnp.bfloat16)
    padded = with_halo(anomaly, (("space", 1),), 1)
    basis_now = balance(padded, balance_coef, sea_float)
    levels = lax.axis_size("tm").bit_length() - 1
    first_level = 0
    other_padded = from_partner(padded, "tm", 0)
    partner = balance(other_padded, balance_coef, sea_float)
    basis_now = merge_pair(basis_now, partner, 0, levels == 1)
    first_level = 1
    for level_idx in range(first_level, levels):
        partner = from_partner(basis_now, "tm", level_idx)
        basis_now = merge_pair(basis_now, partner, level_idx, level_idx == levels - 1)
    return basis_now.reshape(basis_now.shape[0], 3, stored.shape[2], stored.shape[3])


def solution(mesh):
    placed = (P("tm", None, "space", None), P("tm", None), P("space", None), P("space", None))
    return jax.shard_map(
        body, mesh=mesh, in_specs=placed, out_specs=P("tm", None, "space", None), check_vma=False
    )
```

profile of v0, /device:TPU:1, one launch (start us, length us, event | category | flops | bytes accessed | tf_op | source)
XLA Modules:
  0.0 906.1 jit_solution(1723753065468144391)
XLA Ops:
  12.4 5.1 collective-permute-start.1
  33.1 7.0 collective-permute-done.2
  40.1 2.9 fusion.98
  54.2 3.0 fusion.10
  61.3 3.8 fusion.3
  66.2 112.5 %all-reduce.6.cloned.1.call-done = f32[512,256]{1,0:T(8,128)} async-done(((f32[512,256]{1,0:T(8,128)}), f32[512,256]{1,0:T(8,128)}) %all-reduce.6.cloned.1.call-update) | async-done | bytes 524304 | tf_op jit(solution)/shard_map/psum | solution.py:59
  181.2 11.7 %cholesky.214 = f32[128,128]{1,0:T(8,128)S(1)} custom-call(f32[128,128]{1,0:T(8,128)S(1)} %cholesky.346), custom_call_target="Cholesky" | custom-call | tf_op jit(solution)/shard_map/jit(cholesky)/cholesky | solution.py:66
  192.9 9.8 %custom-call.17 = f32[1,128,128]{1,2,0:T(8,128)S(1)} custom-call(f32[1,128,128]{2,1,0:T(8,128)S(1)} %get-tuple-element.118), custom_call_target="InvertDiagBlocksLowerTriangular" | custom-call | tf_op jit(solution)/shard_map/jit(cholesky)/cholesky | solution.py:66
  203.2 11.7 %cholesky.231 = f32[128,128]{1,0:T(8,128)S(1)} custom-call(f32[128,128]{1,0:T(8,128)S(1)} %convolution_subtract_fusion.7), custom_call_target="Cholesky" | custom-call | tf_op jit(solution)/shard_map/jit(cholesky)/cholesky | solution.py:66
  217.7 4.2 while.8
  221.8 19.7 %custom-call.18 = f32[2,128,128]{1,2,0:T(8,128)S(1)} custom-call(f32[2,128,128]{2,1,0:T(8,128)S(1)} %get-tuple-element.33), custom_call_target="InvertDiagBlocksLowerTriangular" | custom-call | tf_op jit(solution)/shard_map/jit(_solve_triangular)/triangular_solve | solution.py:68
  246.8 34.2 %collective-permute-done.3 = bf16[256,3072]{1,0:T(8,128)(2,1)} collective-permute-done((bf16[256,3072]{1,0:T(8,128)(2,1)S(1)}, bf16[256,3072]{1,0:T(8,128)(2,1)}, u32[]{:S(2)}, u32[]{:S(2)}) %collective-permute-start.3) | collective-permute-done | bytes 1572896 | tf_op jit(solution)/shard_map/ppermute | solution.py:31
  286.3 110.5 %all-reduce.8.cloned.1.call-done = f32[512,256]{1,0:T(8,128)} async-done(((f32[512,256]{1,0:T(8,128)}), f32[512,256]{1,0:T(8,128)}) %all-reduce.8.cloned.1.call-update) | async-done | bytes 524304 | tf_op jit(solution)/shard_map/psum | solution.py:59
  399.2 11.7 %cholesky.248 = f32[128,128]{1,0:T(8,128)S(1)} custom-call(f32[128,128]{1,0:T(8,128)S(1)} %cholesky.349), custom_call_target="Cholesky" | custom-call | tf_op jit(solution)/shard_map/jit(cholesky)/cholesky | solution.py:66
  411.0 9.8 %custom-call.19 = f32[1,128,128]{1,2,0:T(8,128)S(1)} custom-call(f32[1,128,128]{2,1,0:T(8,128)S(1)} %get-tuple-element.114), custom_call_target="InvertDiagBlocksLowerTriangular" | custom-call | tf_op jit(solution)/shard_map/jit(cholesky)/cholesky | solution.py:66
  421.3 11.7 %cholesky.265 = f32[128,128]{1,0:T(8,128)S(1)} custom-call(f32[128,128]{1,0:T(8,128)S(1)} %convolution_subtract_fusion.6), custom_call_target="Cholesky" | custom-call | tf_op jit(solution)/shard_map/jit(cholesky)/cholesky | solution.py:66
  435.7 4.1 while.9
  439.8 19.7 %custom-call.20 = f32[2,128,128]{1,2,0:T(8,128)S(1)} custom-call(f32[2,128,128]{2,1,0:T(8,128)S(1)} %get-tuple-element.34), custom_call_target="InvertDiagBlocksLowerTriangular" | custom-call | tf_op jit(solution)/shard_map/jit(_solve_triangular)/triangular_solve | solution.py:68
  464.3 34.4 %collective-permute-done.4 = bf16[256,3072]{1,0:T(8,128)(2,1)} collective-permute-done((bf16[256,3072]{1,0:T(8,128)(2,1)}, bf16[256,3072]{1,0:T(8,128)(2,1)}, u32[]{:S(2)}, u32[]{:S(2)}) %collective-permute-start.4) | collective-permute-done | bytes 1572896 | tf_op jit(solution)/shard_map/ppermute | solution.py:31
  503.8 110.7 %all-reduce.10.cloned.1.call-done = f32[512,256]{1,0:T(8,128)} async-done(((f32[512,256]{1,0:T(8,128)}), f32[512,256]{1,0:T(8,128)}) %all-reduce.10.cloned.1.call-update) | async-done | bytes 524304 | tf_op jit(solution)/shard_map/psum | solution.py:59
  617.0 11.7 %cholesky.282 = f32[128,128]{1,0:T(8,128)S(1)} custom-call(f32[128,128]{1,0:T(8,128)S(1)} %cholesky.352), custom_call_target="Cholesky" | custom-call | tf_op jit(solution)/shard_map/jit(cholesky)/cholesky | solution.py:66
  628.7 9.8 %custom-call.21 = f32[1,128,128]{1,2,0:T(8,128)S(1)} custom-call(f32[1,128,128]{2,1,0:T(8,128)S(1)} %get-tuple-element.110), custom_call_target="InvertDiagBlocksLowerTriangular" | custom-call | tf_op jit(solution)/shard_map/jit(cholesky)/cholesky | solution.py:66
  639.0 11.7 %cholesky.299 = f32[128,128]{1,0:T(8,128)S(1)} custom-call(f32[128,128]{1,0:T(8,128)S(1)} %convolution_subtract_fusion.5), custom_call_target="Cholesky" | custom-call | tf_op jit(solution)/shard_map/jit(cholesky)/cholesky | solution.py:66
  653.4 4.3 while.10
  657.8 19.7 %custom-call.22 = f32[2,128,128]{1,2,0:T(8,128)S(1)} custom-call(f32[2,128,128]{2,1,0:T(8,128)S(1)} %get-tuple-element.35), custom_call_target="InvertDiagBlocksLowerTriangular" | custom-call | tf_op jit(solution)/shard_map/jit(_solve_triangular)/triangular_solve | solution.py:68
  683.8 34.4 %collective-permute-done.5 = bf16[256,3072]{1,0:T(8,128)(2,1)} collective-permute-done((bf16[256,3072]{1,0:T(8,128)(2,1)}, bf16[256,3072]{1,0:T(8,128)(2,1)}, u32[]{:S(2)}, u32[]{:S(2)}) %collective-permute-start.5) | collective-permute-done | bytes 1572896 | tf_op jit(solution)/shard_map/ppermute | solution.py:31
  723.0 111.0 %all-reduce.12.cloned.1.call-done = f32[512,256]{1,0:T(8,128)} async-done(((f32[512,256]{1,0:T(8,128)}), f32[512,256]{1,0:T(8,128)}) %all-reduce.12.cloned.1.call-update) | async-done | bytes 524304 | tf_op jit(solution)/shard_map/psum | solution.py:59
  836.4 11.7 %cholesky.316 = f32[128,128]{1,0:T(8,128)S(1)} custom-call(f32[128,128]{1,0:T(8,128)S(1)} %cholesky.355), custom_call_target="Cholesky" | custom-call | tf_op jit(solution)/shard_map/jit(cholesky)/cholesky | solution.py:66
  848.2 9.8 %custom-call.23 = f32[1,128,128]{1,2,0:T(8,128)S(1)} custom-call(f32[1,128,128]{2,1,0:T(8,128)S(1)} %get-tuple-element.106), custom_call_target="InvertDiagBlocksLowerTriangular" | custom-call | tf_op jit(solution)/shard_map/jit(cholesky)/cholesky | solution.py:66
  858.5 11.9 %cholesky.333 = f32[128,128]{1,0:T(8,128)S(1)} custom-call(f32[128,128]{1,0:T(8,128)S(1)} %convolution_subtract_fusion.4), custom_call_target="Cholesky" | custom-call | tf_op jit(solution)/shard_map/jit(cholesky)/cholesky | solution.py:66
  873.0 3.9 while.11
  877.0 19.7 %custom-call.24 = f32[2,128,128]{1,2,0:T(8,128)S(1)} custom-call(f32[2,128,128]{2,1,0:T(8,128)S(1)} %get-tuple-element.36), custom_call_target="InvertDiagBlocksLowerTriangular" | custom-call | tf_op jit(solution)/shard_map/jit(_solve_triangular)/triangular_solve | solution.py:68
  (193 shorter events, 104.6 us)
Async XLA Ops:
  6.5 172.2 %all-reduce.6.cloned.1.call-start = ((), (), s32[]{:S(2)}) async-start(), calls=%async_computation | async-start | bytes 1048576 | tf_op jit(solution)/shard_map/psum | solution.py:59
  11.9 8.1 copy-start
  12.4 7.6 collective-permute-start.1
  17.5 3.9 collective-permute-start
  23.0 17.1 %collective-permute-start.2 = (bf16[256,10,128]{2,0,1:T(8,128)(2,1)}, bf16[256,10,128]{2,0,1:T(8,128)(2,1)}, u32[]{:S(2)}, u32[]{:S(2)}) collective-permute-start(bf16[256,10,128]{2,0,1:T(8,128)(2,1)} %copy.45), channel_id=1, source_target_pairs={{0,16},{16,0},{32,48},{48,32},{64,80},{80,64},{96,112},{112,96},{1... | collective-permute-start | bytes 1966088 | tf_op jit(solution)/shard_map/ppermute | solution.py:31
  27.1 4.3 copy-start.20
  27.1 4.3 copy-start.21
  50.9 2.4 copy-start.1
  50.9 2.4 copy-start.6
  50.9 2.6 copy-start.7
  50.9 2.9 copy-start.8
  50.9 3.3 copy-start.9
  54.2 3.0 copy-start.10
  59.5 1.9 copy-start.11
  66.0 330.8 %all-reduce.8.cloned.1.call-start = ((), (), s32[]{:S(2)}) async-start(), calls=%async_computation.1 | async-start | bytes 1048576 | tf_op jit(solution)/shard_map/psum | solution.py:59
  181.1 60.4 %copy-start.3 = (f32[512,256]{1,0:T(8,128)S(1)}, f32[512,256]{1,0:T(8,128)}, u32[]{:S(2)}) copy-start(f32[512,256]{1,0:T(8,128)} %all-reduce.6.cloned.1.call-done) | copy-start | bytes 1572868
  241.5 1.5 copy-start.12
  244.0 2.8 copy-start.19
  244.0 37.0 %collective-permute-start.3 = (bf16[256,3072]{1,0:T(8,128)(2,1)S(1)}, bf16[256,3072]{1,0:T(8,128)(2,1)}, u32[]{:S(2)}, u32[]{:S(2)}) collective-permute-start(bf16[256,3072]{1,0:T(8,128)(2,1)S(1)} %convolution_convert_fusion.2), channel_id=1, source_target_pairs={{0,32},{16,48},{32,0},{48,16},{64,96},{80,112},{96,64},{112,80},{1... | collective-permute-start | bytes 4718600 | tf_op jit(solution)/shard_map/ppermute | solution.py:31
  283.1 1.8 copy-start.15
  285.8 328.7 %all-reduce.10.cloned.1.call-start = ((), (), s32[]{:S(2)}) async-start(), calls=%async_computation.2 | async-start | bytes 1048576 | tf_op jit(solution)/shard_map/psum | solution.py:59
  399.2 60.3 %copy-start.4 = (f32[512,256]{1,0:T(8,128)S(1)}, f32[512,256]{1,0:T(8,128)}, u32[]{:S(2)}) copy-start(f32[512,256]{1,0:T(8,128)} %all-reduce.8.cloned.1.call-done) | copy-start | bytes 1572868
  459.5 1.5 copy-start.16
  463.1 35.6 %collective-permute-start.4 = (bf16[256,3072]{1,0:T(8,128)(2,1)}, bf16[256,3072]{1,0:T(8,128)(2,1)}, u32[]{:S(2)}, u32[]{:S(2)}) collective-permute-start(bf16[256,3072]{1,0:T(8,128)(2,1)} %convolution_convert_fusion.1), channel_id=1, source_target_pairs={{0,64},{16,80},{32,96},{48,112},{64,0},{80,16},{96,32},{112,48},{1... | collective-permute-start | bytes 4718600 | tf_op jit(solution)/shard_map/ppermute | solution.py:31
  500.8 1.8 copy-start.17
  503.6 330.4 %all-reduce.12.cloned.1.call-start = ((), (), s32[]{:S(2)}) async-start(), calls=%async_computation.3 | async-start | bytes 1048576 | tf_op jit(solution)/shard_map/psum | solution.py:59
  616.9 60.5 %copy-start.5 = (f32[512,256]{1,0:T(8,128)S(1)}, f32[512,256]{1,0:T(8,128)}, u32[]{:S(2)}) copy-start(f32[512,256]{1,0:T(8,128)} %all-reduce.10.cloned.1.call-done) | copy-start | bytes 1572868
  677.4 1.5 copy-start.18
  681.1 37.1 %collective-permute-start.5 = (bf16[256,3072]{1,0:T(8,128)(2,1)}, bf16[256,3072]{1,0:T(8,128)(2,1)}, u32[]{:S(2)}, u32[]{:S(2)}) collective-permute-start(bf16[256,3072]{1,0:T(8,128)(2,1)} %convolution_convert_fusion), channel_id=1, source_target_pairs={{0,128},{16,144},{32,160},{48,176},{64,192},{80,208},{96,224},{112... | collective-permute-start | bytes 4718600 | tf_op jit(solution)/shard_map/ppermute | solution.py:31
  720.3 1.8 copy-start.13
  836.4 60.3 %copy-start.2 = (f32[512,256]{1,0:T(8,128)S(1)}, f32[512,256]{1,0:T(8,128)}, u32[]{:S(2)}) copy-start(f32[512,256]{1,0:T(8,128)} %all-reduce.12.cloned.1.call-done) | copy-start | bytes 1572868
  896.7 1.5 copy-start.14
Sparse Core Ops, SparseCore 0:
  66.1 112.5 all-reduce.5
  286.0 110.8 all-reduce.7
  503.7 110.8 all-reduce.9
  723.1 110.8 all-reduce.11
where the time goes:
time: 914 us; the launch traced here: 906 us
  waiting for transfers between devices  557 us (61%)
  other arithmetic  241 us (26%)
  local copies, waits for them, and re-layouts  40.6 us (4%)
  matrix products  31.5 us (3%)
  between operations  19.1 us (2%)
  starting transfers between devices  15.7 us (2%)
    psum x4, waiting for transfers between devices, merge_pair(): mixed_cols = lax.psum(local_mixed, 'space')  445 us
    another operation x28, other arithmetic, merge_pair(): factor_low = jnp.linalg.cholesky(normal)  139 us
    ppermute x4, waiting for transfers between devices, from_partner(): lax.ppermute(shard, axis, [(i, i ^ 1 << stride) for i in range(lax.axis_s...  110 us
    another operation x9, other arithmetic, merge_pair(): jax.scipy.linalg.solve_triangular(factor_low, mixed_cols.T, lower=True)  78.8 us
  transfers between devices with their start and end apart: 10, of which 10 were waited for; matrix products, arithmetic and copies ran while one was open for 1% of the time, Pallas kernels for 0%

commit v1 on v0

--- a/solution.py
+++ b/solution.py
@@ -56,7 +56,7 @@
     members = own_basis.shape[0]
     local_gram = jnp.dot(stacked, stacked.T, preferred_element_type=jnp.float32)
     local_mixed = (local_gram[:, :members] + local_gram[:, members:]) * inv_root2
-    mixed_cols = lax.psum(local_mixed, "space")
+    mixed_cols = jnp.sum(lax.all_gather(local_mixed, "space"), axis=0)
     normal = jnp.dot(
         mixed_cols.T,
         mixed_cols,

time: 914 us -> 706 us (0.77)
  waiting for transfers between devices: 557 us -> 337 us
  other arithmetic: 241 us -> 258 us
    psum x4 -> x0, waiting for transfers between devices: 445 us -> none  [merge_pair(): mixed_cols = lax.psum(local_mixed, 'space')]
    all_gather x0 -> x4, waiting for transfers between devices: none -> 224 us  [merge_pair(): mixed_cols = jnp.sum(lax.all_gather(local_mixed, 'space'), axis=0)]
    reduce_sum x0 -> x4, other arithmetic: none -> 15.9 us  [merge_pair(): mixed_cols = jnp.sum(lax.all_gather(local_mixed, 'space'), axis=0)]
where the time goes in v1:
time: 706 us; the launch traced here: 698 us
  waiting for transfers between devices  337 us (48%)
  other arithmetic  258 us (37%)
  local copies, waits for them, and re-layouts  42.1 us (6%)
  matrix products  25.8 us (4%)
  between operations  19.3 us (3%)
  starting transfers between devices  15.5 us (2%)
    all_gather x4, waiting for transfers between devices, merge_pair(): mixed_cols = jnp.sum(lax.all_gather(local_mixed, 'space'), axis=0)  224 us
    another operation x28, other arithmetic, merge_pair(): factor_low = jnp.linalg.cholesky(normal)  139 us
    ppermute x4, waiting for transfers between devices, from_partner(): lax.ppermute(shard, axis, [(i, i ^ 1 << stride) for i in range(lax.axis_s...  111 us
    another operation x9, other arithmetic, merge_pair(): jax.scipy.linalg.solve_triangular(factor_low, mixed_cols.T, lower=True)  79.4 us
    reduce_sum x4, other arithmetic, merge_pair(): mixed_cols = jnp.sum(lax.all_gather(local_mixed, 'space'), axis=0)  15.9 us
    another operation x29, local copies, waits for them, and re-layouts, merge_pair(): jax.scipy.linalg.solve_triangular(factor_low, mixed_cols.T, lower=True)  15.8 us
  transfers between devices with their start and end apart: 10, of which 10 were waited for; matrix products, arithmetic and copies ran while one was open for 1% of the time, Pallas kernels for 0%

profile of v1, /device:TPU:1, one launch (start us, length us, event | category | flops | bytes accessed | tf_op | source)
XLA Modules:
  0.0 697.9 jit_solution(8173415146015990328)
XLA Ops:
  12.4 5.1 collective-permute-start.1
  33.1 7.0 %collective-permute-done.2 = bf16[256,10,128]{2,0,1:T(8,128)(2,1)} collective-permute-done((bf16[256,10,128]{2,0,1:T(8,128)(2,1)}, bf16[256,10,128]{2,0,1:T(8,128)(2,1)}, u32[]{:S(2)}, u32[]{:S(2)}) %collective-permute-start.2) | collective-permute-done | bytes 655392 | tf_op jit(solution)/shard_map/ppermute | solution.py:31
  66.2 58.2 %all-gather.9.cloned.1.call-done = f32[8192,256]{1,0:T(8,128)} async-done(((f32[512,256]{1,0:T(8,128)}), f32[8192,256]{1,0:T(8,128)}) %all-gather.9.cloned.1.call-update) | async-done | bytes 8388624 | tf_op jit(solution)/shard_map/all_gather | solution.py:59
  124.4 4.0 reduce_sum.46
  129.8 11.7 %cholesky.214 = f32[128,128]{1,0:T(8,128)S(1)} custom-call(f32[128,128]{1,0:T(8,128)S(1)} %cholesky.346), custom_call_target="Cholesky" | custom-call | tf_op jit(solution)/shard_map/jit(cholesky)/cholesky | solution.py:66
  141.6 9.8 %custom-call.17 = f32[1,128,128]{1,2,0:T(8,128)S(1)} custom-call(f32[1,128,128]{2,1,0:T(8,128)S(1)} %get-tuple-element.118), custom_call_target="InvertDiagBlocksLowerTriangular" | custom-call | tf_op jit(solution)/shard_map/jit(cholesky)/cholesky | solution.py:66
  151.9 11.7 %cholesky.231 = f32[128,128]{1,0:T(8,128)S(1)} custom-call(f32[128,128]{1,0:T(8,128)S(1)} %convolution_subtract_fusion.7), custom_call_target="Cholesky" | custom-call | tf_op jit(solution)/shard_map/jit(cholesky)/cholesky | solution.py:66
  166.6 3.9 while.8
  170.5 19.7 %custom-call.18 = f32[2,128,128]{1,2,0:T(8,128)S(1)} custom-call(f32[2,128,128]{2,1,0:T(8,128)S(1)} %get-tuple-element.33), custom_call_target="InvertDiagBlocksLowerTriangular" | custom-call | tf_op jit(solution)/shard_map/jit(_solve_triangular)/triangular_solve | solution.py:68
  195.4 34.6 %collective-permute-done.3 = bf16[256,3072]{1,0:T(8,128)(2,1)} collective-permute-done((bf16[256,3072]{1,0:T(8,128)(2,1)S(1)}, bf16[256,3072]{1,0:T(8,128)(2,1)}, u32[]{:S(2)}, u32[]{:S(2)}) %collective-permute-start.3) | collective-permute-done | bytes 1572896 | tf_op jit(solution)/shard_map/ppermute | solution.py:31
  235.3 54.9 %all-gather.11.cloned.1.call-done = f32[8192,256]{1,0:T(8,128)} async-done(((f32[512,256]{1,0:T(8,128)}), f32[8192,256]{1,0:T(8,128)}) %all-gather.11.cloned.1.call-update) | async-done | bytes 8388624 | tf_op jit(solution)/shard_map/all_gather | solution.py:59
  290.2 4.0 reduce_sum.47
  295.6 11.7 %cholesky.248 = f32[128,128]{1,0:T(8,128)S(1)} custom-call(f32[128,128]{1,0:T(8,128)S(1)} %cholesky.349), custom_call_target="Cholesky" | custom-call | tf_op jit(solution)/shard_map/jit(cholesky)/cholesky | solution.py:66
  307.4 9.8 %custom-call.19 = f32[1,128,128]{1,2,0:T(8,128)S(1)} custom-call(f32[1,128,128]{2,1,0:T(8,128)S(1)} %get-tuple-element.114), custom_call_target="InvertDiagBlocksLowerTriangular" | custom-call | tf_op jit(solution)/shard_map/jit(cholesky)/cholesky | solution.py:66
  317.7 11.7 %cholesky.265 = f32[128,128]{1,0:T(8,128)S(1)} custom-call(f32[128,128]{1,0:T(8,128)S(1)} %convolution_subtract_fusion.6), custom_call_target="Cholesky" | custom-call | tf_op jit(solution)/shard_map/jit(cholesky)/cholesky | solution.py:66
  336.2 19.7 %custom-call.20 = f32[2,128,128]{1,2,0:T(8,128)S(1)} custom-call(f32[2,128,128]{2,1,0:T(8,128)S(1)} %get-tuple-element.34), custom_call_target="InvertDiagBlocksLowerTriangular" | custom-call | tf_op jit(solution)/shard_map/jit(_solve_triangular)/triangular_solve | solution.py:68
  360.7 34.8 %collective-permute-done.4 = bf16[256,3072]{1,0:T(8,128)(2,1)} collective-permute-done((bf16[256,3072]{1,0:T(8,128)(2,1)}, bf16[256,3072]{1,0:T(8,128)(2,1)}, u32[]{:S(2)}, u32[]{:S(2)}) %collective-permute-start.4) | collective-permute-done | bytes 1572896 | tf_op jit(solution)/shard_map/ppermute | solution.py:31
  400.3 55.4 %all-gather.13.cloned.1.call-done = f32[8192,256]{1,0:T(8,128)} async-done(((f32[512,256]{1,0:T(8,128)}), f32[8192,256]{1,0:T(8,128)}) %all-gather.13.cloned.1.call-update) | async-done | bytes 8388624 | tf_op jit(solution)/shard_map/all_gather | solution.py:59
  455.7 4.0 reduce_sum.48
  461.1 11.7 %cholesky.282 = f32[128,128]{1,0:T(8,128)S(1)} custom-call(f32[128,128]{1,0:T(8,128)S(1)} %cholesky.352), custom_call_target="Cholesky" | custom-call | tf_op jit(solution)/shard_map/jit(cholesky)/cholesky | solution.py:66
  472.9 9.8 %custom-call.21 = f32[1,128,128]{1,2,0:T(8,128)S(1)} custom-call(f32[1,128,128]{2,1,0:T(8,128)S(1)} %get-tuple-element.110), custom_call_target="InvertDiagBlocksLowerTriangular" | custom-call | tf_op jit(solution)/shard_map/jit(cholesky)/cholesky | solution.py:66
  483.1 11.7 %cholesky.299 = f32[128,128]{1,0:T(8,128)S(1)} custom-call(f32[128,128]{1,0:T(8,128)S(1)} %convolution_subtract_fusion.5), custom_call_target="Cholesky" | custom-call | tf_op jit(solution)/shard_map/jit(cholesky)/cholesky | solution.py:66
  497.9 3.9 while.10
  501.9 19.7 %custom-call.22 = f32[2,128,128]{1,2,0:T(8,128)S(1)} custom-call(f32[2,128,128]{2,1,0:T(8,128)S(1)} %get-tuple-element.35), custom_call_target="InvertDiagBlocksLowerTriangular" | custom-call | tf_op jit(solution)/shard_map/jit(_solve_triangular)/triangular_solve | solution.py:68
  527.8 34.8 %collective-permute-done.5 = bf16[256,3072]{1,0:T(8,128)(2,1)} collective-permute-done((bf16[256,3072]{1,0:T(8,128)(2,1)}, bf16[256,3072]{1,0:T(8,128)(2,1)}, u32[]{:S(2)}, u32[]{:S(2)}) %collective-permute-start.5) | collective-permute-done | bytes 1572896 | tf_op jit(solution)/shard_map/ppermute | solution.py:31
  567.4 55.4 %all-gather.15.cloned.1.call-done = f32[8192,256]{1,0:T(8,128)} async-done(((f32[512,256]{1,0:T(8,128)}), f32[8192,256]{1,0:T(8,128)}) %all-gather.15.cloned.1.call-update) | async-done | bytes 8388624 | tf_op jit(solution)/shard_map/all_gather | solution.py:59
  622.8 4.0 reduce_sum.49
  628.2 11.7 %cholesky.316 = f32[128,128]{1,0:T(8,128)S(1)} custom-call(f32[128,128]{1,0:T(8,128)S(1)} %cholesky.355), custom_call_target="Cholesky" | custom-call | tf_op jit(solution)/shard_map/jit(cholesky)/cholesky | solution.py:66
  640.0 9.8 %custom-call.23 = f32[1,128,128]{1,2,0:T(8,128)S(1)} custom-call(f32[1,128,128]{2,1,0:T(8,128)S(1)} %get-tuple-element.106), custom_call_target="InvertDiagBlocksLowerTriangular" | custom-call | tf_op jit(solution)/shard_map/jit(cholesky)/cholesky | solution.py:66
  650.3 11.9 %cholesky.333 = f32[128,128]{1,0:T(8,128)S(1)} custom-call(f32[128,128]{1,0:T(8,128)S(1)} %convolution_subtract_fusion.4), custom_call_target="Cholesky" | custom-call | tf_op jit(solution)/shard_map/jit(cholesky)/cholesky | solution.py:66
  664.9 4.0 while.11
  668.9 19.7 %custom-call.24 = f32[2,128,128]{1,2,0:T(8,128)S(1)} custom-call(f32[2,128,128]{2,1,0:T(8,128)S(1)} %get-tuple-element.36), custom_call_target="InvertDiagBlocksLowerTriangular" | custom-call | tf_op jit(solution)/shard_map/jit(_solve_triangular)/triangular_solve | solution.py:68
  (193 shorter events, 114.5 us)
Async XLA Ops:
  6.5 117.9 %all-gather.9.cloned.1.call-start = ((), (), s32[]{:S(2)}) async-start(), calls=%async_computation | async-start | bytes 8912896 | tf_op jit(solution)/shard_map/all_gather | solution.py:59
  11.9 8.1 %copy-start = (bf16[256,8,128]{2,1,0:T(8,128)(2,1)}, bf16[256,8,128]{2,1,0:T(8,128)(2,1)S(1)}, u32[]{:S(2)}) copy-start(bf16[256,8,128]{2,1,0:T(8,128)(2,1)S(1)} %gather_fusion) | copy-start | bytes 1572868
  12.4 7.6 %collective-permute-start.1 = (bf16[256,1,128]{2,1,0:T(2,128)(2,1)S(1)}, bf16[256,1,128]{2,1,0:T(2,128)(2,1)S(1)}, u32[]{:S(2)}, u32[]{:S(2)}) collective-permute-start(bf16[256,1,128]{2,1,0:T(2,128)(2,1)S(1)} %get-tuple-element.102), channel_id=1, source_target_pairs={{1,0},{2,1},{3,2},{4,3},{5,4},{6,5},{7,6},{8,7},{9,8},{10,9},{11,1... | collective-permute-start | bytes 196616 | tf_op jit(solution)/shard_map/ppermute | solution.py:23
  17.5 3.9 collective-permute-start
  23.0 17.1 %collective-permute-start.2 = (bf16[256,10,128]{2,0,1:T(8,128)(2,1)}, bf16[256,10,128]{2,0,1:T(8,128)(2,1)}, u32[]{:S(2)}, u32[]{:S(2)}) collective-permute-start(bf16[256,10,128]{2,0,1:T(8,128)(2,1)} %copy.41), channel_id=1, source_target_pairs={{0,16},{16,0},{32,48},{48,32},{64,80},{80,64},{96,112},{112,96},{1... | collective-permute-start | bytes 1966088 | tf_op jit(solution)/shard_map/ppermute | solution.py:31
  27.1 4.3 copy-start.16
  27.1 4.3 copy-start.17
  50.8 2.4 copy-start.1
  50.9 2.4 copy-start.2
  50.9 2.6 copy-start.3
  50.9 2.9 copy-start.4
  50.9 3.3 copy-start.5
  54.1 3.0 copy-start.6
  59.5 1.9 copy-start.7
  66.0 224.3 %all-gather.11.cloned.1.call-start = ((), (), s32[]{:S(2)}) async-start(), calls=%async_computation.1 | async-start | bytes 8912896 | tf_op jit(solution)/shard_map/all_gather | solution.py:59
  190.2 1.4 copy-start.8
  192.6 2.8 copy-start.15
  192.6 37.4 %collective-permute-start.3 = (bf16[256,3072]{1,0:T(8,128)(2,1)S(1)}, bf16[256,3072]{1,0:T(8,128)(2,1)}, u32[]{:S(2)}, u32[]{:S(2)}) collective-permute-start(bf16[256,3072]{1,0:T(8,128)(2,1)S(1)} %convolution_convert_fusion.2), channel_id=1, source_target_pairs={{0,32},{16,48},{32,0},{48,16},{64,96},{80,112},{96,64},{112,80},{1... | collective-permute-start | bytes 4718600 | tf_op jit(solution)/shard_map/ppermute | solution.py:31
  232.1 1.8 copy-start.11
  234.8 220.8 %all-gather.13.cloned.1.call-start = ((), (), s32[]{:S(2)}) async-start(), calls=%async_computation.2 | async-start | bytes 8912896 | tf_op jit(solution)/shard_map/all_gather | solution.py:59
  355.9 1.4 copy-start.12
  359.5 36.0 %collective-permute-start.4 = (bf16[256,3072]{1,0:T(8,128)(2,1)}, bf16[256,3072]{1,0:T(8,128)(2,1)}, u32[]{:S(2)}, u32[]{:S(2)}) collective-permute-start(bf16[256,3072]{1,0:T(8,128)(2,1)} %convolution_convert_fusion.1), channel_id=1, source_target_pairs={{0,64},{16,80},{32,96},{48,112},{64,0},{80,16},{96,32},{112,48},{1... | collective-permute-start | bytes 4718600 | tf_op jit(solution)/shard_map/ppermute | solution.py:31
  397.5 1.8 copy-start.13
  400.3 222.6 %all-gather.15.cloned.1.call-start = ((), (), s32[]{:S(2)}) async-start(), calls=%async_computation.3 | async-start | bytes 8912896 | tf_op jit(solution)/shard_map/all_gather | solution.py:59
  521.6 1.4 copy-start.14
  525.1 37.5 %collective-permute-start.5 = (bf16[256,3072]{1,0:T(8,128)(2,1)}, bf16[256,3072]{1,0:T(8,128)(2,1)}, u32[]{:S(2)}, u32[]{:S(2)}) collective-permute-start(bf16[256,3072]{1,0:T(8,128)(2,1)} %convolution_convert_fusion), channel_id=1, source_target_pairs={{0,128},{16,144},{32,160},{48,176},{64,192},{80,208},{96,224},{112... | collective-permute-start | bytes 4718600 | tf_op jit(solution)/shard_map/ppermute | solution.py:31
  564.7 1.8 copy-start.9
  688.6 1.4 copy-start.10
Sparse Core Ops, SparseCore 0:
  66.1 58.2 all-gather.8
  234.9 55.2 all-gather.10
  400.4 55.2 all-gather.12
  567.6 55.2 all-gather.14
